TPU v7x, 256 devices: a whole 4x4x8 slice. The times are simulated.
256 devices in a mesh: wide: 32 (over z_hi, y, core), narrow: 8 (over z_lo, x).
Axes of the slice: x: 4, y: 4, z: 8 (z_hi: 4, z_lo: 2; z = z_hi * 2 + z_lo), core: 2. Of those that a mesh axis runs over, the one named last changes fastest.
Arguments:
- residual: bfloat16 [256, 8192], P('wide'), may hold values from -60 to 60
- norm_gain: float32 [8192], replicated, may hold values from 0.1 to 1.9
- w_query: bfloat16 [8192, 8192], P('wide', 'narrow'), may hold values from -0.0625 to 0.0625
- key_projection_weight: bfloat16 [8192, 1024], P('wide', 'narrow'), may hold values from -0.0625 to 0.0625
- value_projection_weight: bfloat16 [8192, 1024], P('wide', 'narrow'), may hold values from -0.0625 to 0.0625
- w_out: bfloat16 [8192, 8192], P('narrow', 'wide'), may hold values from -0.5 to 0.5
- cache_keys: bfloat16 [256, 8, 1024, 128], P('wide', 'narrow'), may hold values from -480 to 480
- stored_values: bfloat16 [256, 8, 1024, 128], P('wide', 'narrow'), may hold values from -24 to 24
- lengths: int32 [256], P('wide'), may hold values from 1 to 1024, as said below
- w_enc: bfloat16 [8192, 65536], P('narrow', 'wide'), may hold values from -0.0625 to 0.0625
- b_enc: float32 [65536], P('wide'), may hold values from -3 to 3
- w_dec: bfloat16 [65536, 8192], P('wide', 'narrow'), may hold values from -0.0625 to 0.0625
- b_dec: float32 [8192], P('narrow'), may hold values from -3 to 3
- clamp_index: int32 [256, 8], replicated, may hold values from 0 to 65535, as said below
- clamp_value: float32 [256, 8], replicated, may hold values from 10 to 40
Outputs:
- steered: bfloat16 [256, 8192], P('wide', 'narrow')
Inputs may be any that keep to these rules, and one draw needn't show every extreme that they name: `lengths`: row 0 has all 1024 slots filled. `clamp_index`: the 8 latents of a row are distinct.
All inputs are finite; a program needn't handle non-finite values.
Results may differ from a plain program's by a relative error of at most 0.014.
The roundings to bfloat16 on the way count: a program that leaves them out, or rounds other values in their place, can miss the bound.
Values may be sent and summed in bfloat16 or wider, within the bound.
No kernel may reach another device: no remote copies, remote signals or barrier semaphores. Data moves between devices by JAX's collectives and lax.ppermute only.
A program may use at most 64 MiB of HBM per device.

v0:
```python
import math
import jax
import jax.numpy as jnp
from jax import lax
from jax.sharding import PartitionSpec as P

HEAD_WIDTH = 128
rope_base = 500000.0


def rotary(vectors, positions):
    halfway = vectors.shape[-1] // 2
    counter = jnp.arange(halfway, dtype=jnp.float32)
    inverse = rope_base ** (-2.0 * counter / vectors.shape[-1])
    angles = positions.astype(jnp.float32)[:, None] * inverse[None, :]
    cosine = jnp.cos(angles)[:, None, :]
    sine = jnp.sin(angles)[:, None, :]
    first_half = vectors[..., :halfway]
    second_half = vectors[..., halfway:]
    return jnp.concatenate(
        [first_half * cosine - second_half * sine, second_half * cosine + first_half * sine],
        axis=-1,
    )


def clamp_latents(pre_acts, latent_first, clamp_index, clamp_value):
    columns = latent_first + jnp.arange(pre_acts.shape[1], dtype=jnp.int32)
    result = jnp.maximum(pre_acts, 0.0)
    for clamp_slot in range(clamp_index.shape[1]):
        matched = columns[None, :] == clamp_index[:, clamp_slot : clamp_slot + 1]
        result = jnp.where(matched, clamp_value[:, clamp_slot : clamp_slot + 1], result)
    return result.astype(jnp.bfloat16)


def attend(queries, key_new, value_new, cache_keys, stored_values, lengths):
    local_rows, heads_here, head_size = queries.shape
    kv_here = key_new.shape[1]
    query_group_width = heads_here // kv_here
    grouped_queries = queries.reshape(local_rows, kv_here, query_group_width, head_size)
    scaling = 1.0 / math.sqrt(head_size)
    scores = (
        jnp.einsum(
            "rkgd,rkjd->rkgj", grouped_queries, cache_keys, preferred_element_type=jnp.float32
        )
        * scaling
    )
    in_range = (
        jnp.arange(cache_keys.shape[2], dtype=jnp.int32)[None, None, None, :]
        < lengths[:, None, None, None]
    )
    scores = jnp.where(in_range, scores, -jnp.inf)
    own_score = (
        jnp.einsum("rkgd,rkd->rkg", grouped_queries, key_new, preferred_element_type=jnp.float32)
        * scaling
    )
    highest = jnp.maximum(jnp.max(scores, axis=-1), own_score)
    weights = jnp.exp(scores - highest[..., None])
    own_weight = jnp.exp(own_score - highest)
    denominator = jnp.sum(weights, axis=-1) + own_weight
    probabilities = (weights / denominator[..., None]).astype(jnp.bfloat16)
    own_prob = (own_weight / denominator).astype(jnp.bfloat16)
    blended = jnp.einsum(
        "rkgj,rkjd->rkgd", probabilities, stored_values, preferred_element_type=jnp.float32
    )
    blended = (
        blended
        + own_prob.astype(jnp.float32)[..., None] * value_new.astype(jnp.float32)[:, :, None, :]
    )
    return blended.astype(jnp.bfloat16).reshape(local_rows, heads_here * head_size)


def on_device(
    residual,
    norm_gain,
    w_query,
    key_projection_weight,
    value_projection_weight,
    w_out,
    cache_keys,
    stored_values,
    lengths,
    w_enc,
    b_enc,
    w_dec,
    b_dec,
    clamp_index,
    clamp_value,
):
    stream = residual.astype(jnp.float32)
    local_rows = residual.shape[0]
    normalized_rows = (
        stream
        * lax.rsqrt(jnp.mean(stream * stream, axis=-1, keepdims=True) + 1e-05)
        * norm_gain[None, :]
    ).astype(jnp.bfloat16)
    by_feature = lax.all_to_all(normalized_rows, "wide", split_axis=1, concat_axis=0, tiled=True)
    query_width = w_query.shape[1]
    key_width = key_projection_weight.shape[1]
    row_block = by_feature
    projected = lax.psum_scatter(
        jnp.concatenate(
            [
                jnp.dot(row_block, w_query, preferred_element_type=jnp.float32),
                jnp.dot(row_block, key_projection_weight, preferred_element_type=jnp.float32),
                jnp.dot(row_block, value_projection_weight, preferred_element_type=jnp.float32),
            ],
            axis=1,
        ),
        "wide",
        scatter_dimension=0,
        tiled=True,
    )
    heads_here = query_width // HEAD_WIDTH
    kv_here = key_width // HEAD_WIDTH
    queries = rotary(
        projected[:, :query_width].reshape(local_rows, heads_here, HEAD_WIDTH), lengths
    ).astype(jnp.bfloat16)
    key_new = rotary(
        projected[:, query_width : query_width + key_width].reshape(
            local_rows, kv_here, HEAD_WIDTH
        ),
        lengths,
    ).astype(jnp.bfloat16)
    value_new = (
        projected[:, query_width + key_width :]
        .reshape(local_rows, kv_here, HEAD_WIDTH)
        .astype(jnp.bfloat16)
    )
    attended = attend(queries, key_new, value_new, cache_keys, stored_values, lengths)
    partial_out = jnp.dot(
        lax.all_gather(attended, "wide", axis=0, tiled=True),
        w_out,
        preferred_element_type=jnp.float32,
    )
    by_row = lax.all_to_all(partial_out, "wide", split_axis=0, concat_axis=1, tiled=True)
    head_total = lax.psum_scatter(by_row, "narrow", scatter_dimension=1, tiled=True)
    width_here = w_enc.shape[0]
    narrow_index = lax.axis_index("narrow")
    own_stream = lax.dynamic_slice_in_dim(stream, narrow_index * width_here, width_here, 1)
    hidden = (own_stream + head_total).astype(jnp.bfloat16)
    partial_pre = jnp.dot(
        lax.all_gather(hidden, "wide", axis=0, tiled=True),
        w_enc,
        preferred_element_type=jnp.float32,
    )
    latents_here = w_enc.shape[1]
    latent_first = lax.axis_index("wide") * latents_here
    summed_pre = lax.psum(partial_pre, "narrow")
    activations = clamp_latents(summed_pre + b_enc[None, :], latent_first, clamp_index, clamp_value)
    row_block = activations
    rebuilt = lax.psum_scatter(
        jnp.dot(row_block, w_dec, preferred_element_type=jnp.float32),
        "wide",
        scatter_dimension=0,
        tiled=True,
    )
    return (rebuilt + b_dec[None, :]).astype(jnp.bfloat16)


def solution(mesh):
    placed = (
        P("wide", None),
        P(),
        P("wide", "narrow"),
        P("wide", "narrow"),
        P("wide", "narrow"),
        P("narrow", "wide"),
        P("wide", "narrow", None, None),
        P("wide", "narrow", None, None),
        P("wide"),
        P("narrow", "wide"),
        P("wide"),
        P("wide", "narrow"),
        P("narrow"),
        P(),
        P(),
    )
    return jax.shard_map(
        on_device, mesh=mesh, in_specs=placed, out_specs=P("wide", "narrow"), check_vma=False
    )
```

profile of v0, /device:TPU:2, one launch (start us, length us, event | category | flops | bytes accessed | tf_op | source)
XLA Modules:
  0.0 458.9 jit_solution(15226275381327403887)
XLA Ops:
  6.5 0.0 copy-start
  6.5 0.0 reduce-scatter.4.cloned.1.call-start
  6.5 1.2 multiply_reduce_fusion
  7.8 1.0 multiply_convert_fusion
  8.8 22.2 %all_to_all.38 = bf16[8,32,256]{2,0,1:T(8,128)(2,1)S(1)} all-to-all(bf16[8,32,256]{2,0,1:T(8,128)(2,1)S(1)} %bitcast.75), channel_id=1, replica_groups=mesh['wide'=32,'narrow'=8] {'wide'}, dimensions={1} | all-to-all | bytes 262144 | tf_op jit(solution)/shard_map/all_to_all | solution.py:96
  31.0 1.3 fusion.44
  32.4 0.0 copy-done.4
  32.4 0.2 fusion.40
  32.6 0.0 copy-done.5
  32.6 0.0 copy-start.9
  32.6 0.2 fusion.42
  32.8 1.2 pad_maximum_fusion
  34.0 0.0 reduce-scatter.4.cloned.1.call-update
  34.0 0.0 reduce-scatter.6.cloned.1.call-start
  34.0 0.0 copy-done.9
  34.1 0.1 iota_compare_fusion
  34.2 0.1 multiply_cosine_fusion.1
  34.3 85.1 %reduce-scatter.4.cloned.1.call-done = f32[8,1280]{1,0:T(8,128)} async-done(((f32[256,1280]{1,0:T(8,128)}), f32[8,1280]{1,0:T(8,128)}) %reduce-scatter.4.cloned.1.call-update) | async-done | bytes 40976 | tf_op jit(solution)/shard_map/reduce_scatter | solution.py:100
  119.4 0.9 slice_bitcast_fusion
  120.3 0.1 fusion.66
  120.4 0.7 slice_bitcast_fusion.1
  121.0 0.1 fusion.61
  121.2 0.1 maximum_bitcast_fusion
  121.3 0.2 fusion.56
  121.5 0.8 fusion.69
  122.2 0.2 fusion.39
  122.5 0.7 fusion.59
  123.1 0.4 fusion.16
  123.6 44.2 %all_gather.6 = bf16[256,1024]{1,0:T(8,128)(2,1)S(1)} all-gather(bf16[8,1024]{1,0:T(8,128)(2,1)S(1)} %bitcast.76), channel_id=1, replica_groups=mesh['wide'=32,'narrow'=8] {'wide'}, dimensions={0}, use_global_device_ids=true | all-gather | bytes 540672 | tf_op jit(solution)/shard_map/all_gather | solution.py:131
  167.8 0.3 convolution_bitcast_fusion
  168.1 17.8 %all_to_all.39 = f32[32,8,256]{2,1,0:T(8,128)} all-to-all(f32[32,8,256]{2,1,0:T(8,128)S(1)} %convolution_bitcast_fusion), channel_id=1, replica_groups=mesh['wide'=32,'narrow'=8] {'wide'}, dimensions={0} | all-to-all | bytes 524288 | tf_op jit(solution)/shard_map/all_to_all | solution.py:135
  185.9 0.0 reduce-scatter.6.cloned.1.call-update
  185.9 0.0 all-reduce.2.cloned.1.call-start
  186.0 33.6 %reduce-scatter.6.cloned.1.call-done = f32[8,1024]{1,0:T(8,128)} async-done(((f32[8,8192]{1,0:T(8,128)}), f32[8,1024]{1,0:T(8,128)}) %reduce-scatter.6.cloned.1.call-update) | async-done | bytes 32784 | tf_op jit(solution)/shard_map/reduce_scatter | solution.py:136
  219.6 0.8 add_convert_fusion.1
  220.4 46.2 %all_gather.7 = bf16[256,1024]{1,0:T(8,128)(2,1)S(1)} all-gather(bf16[8,1024]{1,0:T(8,128)(2,1)S(1)} %add_convert_fusion.1), channel_id=1, replica_groups=mesh['wide'=32,'narrow'=8] {'wide'}, dimensions={0}, use_global_device_ids=true | all-gather | bytes 540672 | tf_op jit(solution)/shard_map/all_gather | solution.py:142
  266.6 4.8 %fusion.70 = f32[256,2048]{1,0:T(8,128)} fusion(bf16[256,1024]{1,0:T(8,128)(2,1)S(1)} %all_gather.7, bf16[1024,2048]{1,0:T(8,128)(2,1)} %param.24), kind=kOutput, calls=%fused_computation.88 | convolution fusion | flops 1073741824 | bytes 6815744 | tf_op jit(solution)/shard_map/dot_general | solution.py:141
  271.4 0.0 all-reduce.2.cloned.1.call-update
  271.4 0.0 reduce-scatter.8.cloned.1.call-start
  271.5 0.6 copy-done.6
  272.1 0.0 copy-done.7
  272.1 82.1 %all-reduce.2.cloned.1.call-done = f32[256,2048]{1,0:T(8,128)} async-done(((f32[256,2048]{1,0:T(8,128)}), f32[256,2048]{1,0:T(8,128)}) %all-reduce.2.cloned.1.call-update) | async-done | bytes 2097168 | tf_op jit(solution)/shard_map/psum | solution.py:148
  354.3 0.0 copy-done.10
  354.3 6.1 %fusion.19 = f32[256,1024]{1,0:T(8,128)} fusion(bf16[2048,1024]{1,0:T(8,128)(2,1)} %param.26, f32[256,2048]{1,0:T(8,128)} %all-reduce.2.cloned.1.call-done, f32[2048]{0:T(1024)S(1)} %copy-done.10, f32[256]{0:T(256)S(1)} %bitcast.93, f32[256]{0:T(256)S(1)} %bitcast.94, f32[256]{0:T(256)S(1)} %bitcast.88, f32[256]{0:T(256)S(1)} %bitcast.89, ...), kind=kOutput, calls=%fused_computation.12 | convolution fusion | flops 1083179008 | bytes 7372800 | tf_op jit(solution)/shard_map/dot_general | solution.py:152
  360.4 0.0 reduce-scatter.8.cloned.1.call-update
  360.4 90.6 %reduce-scatter.8.cloned.1.call-done = f32[8,1024]{1,0:T(8,128)} async-done(((f32[256,1024]{1,0:T(8,128)}), f32[8,1024]{1,0:T(8,128)}) %reduce-scatter.8.cloned.1.call-update) | async-done | bytes 32784 | tf_op jit(solution)/shard_map/reduce_scatter | solution.py:151
  451.0 0.0 copy-done.8
  451.0 1.4 add_convert_fusion
  (24 shorter events, 0.1 us)
Async XLA Ops:
  6.5 114.9 %copy-start = (bf16[8,1,1024,128]{3,2,1,0:T(8,128)(2,1)S(1)}, bf16[8,1,1024,128]{3,2,1,0:T(8,128)(2,1)}, u32[]{:S(2)}) copy-start(bf16[8,1,1024,128]{3,2,1,0:T(8,128)(2,1)} %param.21) | copy-start | bytes 6291460
  6.5 25.8 %copy-start.4 = (bf16[256,128]{1,0:T(8,128)(2,1)S(1)}, bf16[256,128]{1,0:T(8,128)(2,1)}, u32[]{:S(2)}) copy-start(bf16[256,128]{1,0:T(8,128)(2,1)} %param.19) | copy-start | bytes 196612
  6.5 26.0 %copy-start.5 = (bf16[256,128]{1,0:T(8,128)(2,1)S(1)}, bf16[256,128]{1,0:T(8,128)(2,1)}, u32[]{:S(2)}) copy-start(bf16[256,128]{1,0:T(8,128)(2,1)} %param.18) | copy-start | bytes 196612
  6.5 112.8 %reduce-scatter.4.cloned.1.call-start = ((), (), s32[]{:S(2)}) async-start(), calls=%async_computation.5 | async-start | bytes 1351680 | tf_op jit(solution)/shard_map/reduce_scatter | solution.py:100
  32.6 1.5 copy-start.9
  34.0 185.6 %reduce-scatter.6.cloned.1.call-start = ((), (), s32[]{:S(2)}) async-start(), calls=%async_computation.6 | async-start | bytes 294912 | tf_op jit(solution)/shard_map/reduce_scatter | solution.py:136
  119.4 3.8 copy-start.1
  122.2 45.5 %copy-start.3 = (bf16[1024,256]{1,0:T(8,128)(2,1)S(1)}, bf16[1024,256]{1,0:T(8,128)(2,1)}, u32[]{:S(2)}) copy-start(bf16[1024,256]{1,0:T(8,128)(2,1)} %param.20) | copy-start | bytes 1572868
  123.1 62.8 %copy-start.2 = (bf16[8,8192]{1,0:T(8,128)(2,1)S(1)}, bf16[8,8192]{1,0:T(8,128)(2,1)}, u32[]{:S(2)}) copy-start(bf16[8,8192]{1,0:T(8,128)(2,1)} %param.15) | copy-start | bytes 393220
  185.9 168.4 %all-reduce.2.cloned.1.call-start = ((), (), s32[]{:S(2)}) async-start(), calls=%async_computation.7 | async-start | bytes 4194304 | tf_op jit(solution)/shard_map/psum | solution.py:148
  271.4 0.7 copy-start.6
  271.4 0.7 copy-start.7
  271.4 82.9 %copy-start.10 = (f32[2048]{0:T(1024)S(1)}, f32[2048]{0:T(1024)}, u32[]{:S(2)}) copy-start(f32[2048]{0:T(1024)} %param.25) | copy-start | bytes 24580
  271.4 179.6 %reduce-scatter.8.cloned.1.call-start = ((), (), s32[]{:S(2)}) async-start(), calls=%async_computation.8 | async-start | bytes 1081344 | tf_op jit(solution)/shard_map/reduce_scatter | solution.py:151
  354.3 96.7 %copy-start.8 = (f32[1024]{0:T(1024)S(1)}, f32[1024]{0:T(1024)}, u32[]{:S(2)}) copy-start(f32[1024]{0:T(1024)} %param.27) | copy-start | bytes 12292
Sparse Core Ops, SparseCore 0:
  34.1 85.2 reduce-scatter.3
  186.0 33.5 reduce-scatter.5
  271.5 82.6 all-reduce.1
  360.5 90.4 reduce-scatter.7
where the time goes:
time: 459 us
  waiting for transfers between devices  292 us (64%)
  blocking collectives  130 us (28%)
  matrix products  14.3 us (3%)
  between operations  13.3 us (3%)
  other arithmetic  6.94 us (2%)
    reduce_scatter x1, waiting for transfers between devices, on_device(): lax.psum_scatter(jnp.dot(row_block, w_dec, preferred_element_type=jnp.flo...  90.6 us
    reduce_scatter x1, waiting for transfers between devices, on_device(): lax.psum_scatter(jnp.concatenate([jnp.dot(row_block, w_query, preferred_e...  85.1 us
    psum x1, waiting for transfers between devices, on_device(): summed_pre = lax.psum(partial_pre, 'narrow')  82.1 us
    all_gather x1, blocking collectives, on_device(): lax.all_gather(hidden, 'wide', axis=0, tiled=True)  46.2 us
    all_gather x1, blocking collectives, on_device(): lax.all_gather(attended, 'wide', axis=0, tiled=True)  44.2 us
    reduce_scatter x1, waiting for transfers between devices, on_device(): lax.psum_scatter(by_row, 'narrow', scatter_dimension=1, tiled=True)  33.6 us
    all_to_all x1, blocking collectives, on_device(): lax.all_to_all(normalized_rows, 'wide', split_axis=1, concat_axis=0, tile...  22.2 us
    all_to_all x1, blocking collectives, on_device(): lax.all_to_all(partial_out, 'wide', split_axis=0, concat_axis=1, tiled=True)  17.8 us
  transfers between devices with their start and end apart: 4, of which 4 were waited for; matrix products, arithmetic and copies ran while one was open for 0% of the time, Pallas kernels for 0%

commit v1 on v0

--- a/solution.py
+++ b/solution.py
@@ -139,7 +139,9 @@
     own_stream = lax.dynamic_slice_in_dim(stream, narrow_index * width_here, width_here, 1)
     hidden = (own_stream + head_total).astype(jnp.bfloat16)
     partial_pre = jnp.dot(
-        lax.all_gather(hidden, "wide", axis=0, tiled=True),
+        jnp.concatenate(
+            lax.all_to_all(jnp.stack([hidden] * lax.axis_size("wide")), "wide", 0, 0), axis=0
+        ),
         w_enc,
         preferred_element_type=jnp.float32,
     )

time: 459 us -> 442 us (0.963)
  blocking collectives: 130 us -> 110 us
    all_gather x1 -> x0, blocking collectives: 46.2 us -> none  [on_device(): lax.all_gather(hidden, 'wide', axis=0, tiled=True)]
    all_to_all x0 -> x1, blocking collectives: none -> 26.3 us  [on_device(): lax.all_to_all(jnp.stack([hidden] * lax.axis_size('wide')), 'wide', 0, 0)]
where the time goes in v1:
time: 442 us; the launch traced here: 441 us
  waiting for transfers between devices  294 us (67%)
  blocking collectives  110 us (25%)
  matrix products  14.3 us (3%)
  between operations  13.3 us (3%)
  other arithmetic  6.94 us (2%)
    reduce_scatter x1, waiting for transfers between devices, on_device(): lax.psum_scatter(jnp.dot(row_block, w_dec, preferred_element_type=jnp.flo...  90.6 us
    reduce_scatter x1, waiting for transfers between devices, on_device(): lax.psum_scatter(jnp.concatenate([jnp.dot(row_block, w_query, preferred_e...  85.1 us
    psum x1, waiting for transfers between devices, on_device(): summed_pre = lax.psum(partial_pre, 'narrow')  84.3 us
    all_gather x1, blocking collectives, on_device(): lax.all_gather(attended, 'wide', axis=0, tiled=True)  44.2 us
    reduce_scatter x1, waiting for transfers between devices, on_device(): lax.psum_scatter(by_row, 'narrow', scatter_dimension=1, tiled=True)  33.6 us
    all_to_all x1, blocking collectives, on_device(): lax.all_to_all(jnp.stack([hidden] * lax.axis_size('wide')), 'wide', 0, 0)  26.3 us
    all_to_all x1, blocking collectives, on_device(): lax.all_to_all(normalized_rows, 'wide', split_axis=1, concat_axis=0, tile...  22.2 us
    all_to_all x1, blocking collectives, on_device(): lax.all_to_all(partial_out, 'wide', split_axis=0, concat_axis=1, tiled=True)  17.8 us
  transfers between devices with their start and end apart: 4, of which 4 were waited for; matrix products, arithmetic and copies ran while one was open for 0% of the time, Pallas kernels for 0%

profile of v1, /device:TPU:2, one launch (start us, length us, event | category | flops | bytes accessed | tf_op | source)
XLA Modules:
  0.0 441.2 jit_solution(5071816154270145934)
XLA Ops:
  6.5 0.0 copy-start
  6.5 0.0 reduce-scatter.4.cloned.1.call-start
  6.5 1.2 multiply_reduce_fusion
  7.8 1.0 multiply_convert_fusion
  8.8 22.2 %all_to_all.43 = bf16[8,32,256]{2,0,1:T(8,128)(2,1)S(1)} all-to-all(bf16[8,32,256]{2,0,1:T(8,128)(2,1)S(1)} %bitcast.77), channel_id=1, replica_groups=mesh['wide'=32,'narrow'=8] {'wide'}, dimensions={1} | all-to-all | bytes 262144 | tf_op jit(solution)/shard_map/all_to_all | solution.py:96
  31.0 1.3 fusion.46
  32.4 0.0 copy-done.4
  32.4 0.2 fusion.42
  32.6 0.0 copy-start.9
  32.6 0.2 fusion.44
  32.8 1.2 pad_maximum_fusion
  34.0 0.0 reduce-scatter.4.cloned.1.call-update
  34.0 0.0 reduce-scatter.6.cloned.1.call-start
  34.0 0.0 copy-done.9
  34.1 0.1 iota_compare_fusion
  34.2 0.1 multiply_cosine_fusion.1
  34.3 85.1 %reduce-scatter.4.cloned.1.call-done = f32[8,1280]{1,0:T(8,128)} async-done(((f32[256,1280]{1,0:T(8,128)}), f32[8,1280]{1,0:T(8,128)}) %reduce-scatter.4.cloned.1.call-update) | async-done | bytes 40976 | tf_op jit(solution)/shard_map/reduce_scatter | solution.py:100
  119.4 0.9 slice_bitcast_fusion
  120.3 0.1 fusion.68
  120.4 0.7 slice_bitcast_fusion.1
  121.0 0.1 fusion.63
  121.2 0.1 maximum_bitcast_fusion
  121.3 0.2 fusion.58
  121.5 0.8 fusion.71
  122.2 0.2 fusion.41
  122.5 0.7 fusion.61
  123.1 0.4 fusion.16
  123.6 44.2 %all_gather.3 = bf16[256,1024]{1,0:T(8,128)(2,1)S(1)} all-gather(bf16[8,1024]{1,0:T(8,128)(2,1)S(1)} %bitcast.78), channel_id=1, replica_groups=mesh['wide'=32,'narrow'=8] {'wide'}, dimensions={0}, use_global_device_ids=true | all-gather | bytes 540672 | tf_op jit(solution)/shard_map/all_gather | solution.py:131
  167.8 0.3 convolution_bitcast_fusion
  168.1 17.8 %all_to_all.44 = f32[32,8,256]{2,1,0:T(8,128)} all-to-all(f32[32,8,256]{2,1,0:T(8,128)S(1)} %convolution_bitcast_fusion), channel_id=1, replica_groups=mesh['wide'=32,'narrow'=8] {'wide'}, dimensions={0} | all-to-all | bytes 524288 | tf_op jit(solution)/shard_map/all_to_all | solution.py:135
  185.9 0.0 reduce-scatter.6.cloned.1.call-update
  185.9 0.0 all-reduce.2.cloned.1.call-start
  186.0 33.6 %reduce-scatter.6.cloned.1.call-done = f32[8,1024]{1,0:T(8,128)} async-done(((f32[8,8192]{1,0:T(8,128)}), f32[8,1024]{1,0:T(8,128)}) %reduce-scatter.6.cloned.1.call-update) | async-done | bytes 32784 | tf_op jit(solution)/shard_map/reduce_scatter | solution.py:136
  219.6 0.8 add_convert_fusion.1
  220.4 0.1 stack.2
  220.4 26.3 %all_to_all.45 = bf16[32,8,1024]{2,1,0:T(8,128)(2,1)S(1)} all-to-all(bf16[32,8,1024]{2,1,0:T(8,128)(2,1)S(1)} %stack.2), channel_id=1, replica_groups=mesh['wide'=32,'narrow'=8] {'wide'}, dimensions={0} | all-to-all | bytes 1048576 | tf_op jit(solution)/shard_map/all_to_all | solution.py:143
  246.7 4.8 %fusion.39 = f32[256,2048]{1,0:T(8,128)} fusion(bf16[1024,2048]{1,0:T(8,128)(2,1)} %param.24, bf16[32,8,1024]{2,1,0:T(8,128)(2,1)S(1)} %all_to_all.45), kind=kOutput, calls=%fused_computation.32 | convolution fusion | flops 1073741824 | bytes 6815744 | tf_op jit(solution)/shard_map/dot_general | solution.py:141
  251.5 0.0 all-reduce.2.cloned.1.call-update
  251.5 0.0 reduce-scatter.8.cloned.1.call-start
  251.6 0.6 copy-done.6
  252.2 0.0 copy-done.7
  252.2 84.3 %all-reduce.2.cloned.1.call-done = f32[256,2048]{1,0:T(8,128)} async-done(((f32[256,2048]{1,0:T(8,128)}), f32[256,2048]{1,0:T(8,128)}) %all-reduce.2.cloned.1.call-update) | async-done | bytes 2097168 | tf_op jit(solution)/shard_map/psum | solution.py:150
  336.6 0.0 copy-done.10
  336.6 6.1 %fusion.19 = f32[256,1024]{1,0:T(8,128)} fusion(bf16[2048,1024]{1,0:T(8,128)(2,1)} %param.26, f32[256,2048]{1,0:T(8,128)} %all-reduce.2.cloned.1.call-done, f32[2048]{0:T(1024)S(1)} %copy-done.10, f32[256]{0:T(256)S(1)} %bitcast.95, f32[256]{0:T(256)S(1)} %bitcast.96, f32[256]{0:T(256)S(1)} %bitcast.90, f32[256]{0:T(256)S(1)} %bitcast.91, ...), kind=kOutput, calls=%fused_computation.12 | convolution fusion | flops 1083179008 | bytes 7372800 | tf_op jit(solution)/shard_map/dot_general | solution.py:154
  342.7 0.0 reduce-scatter.8.cloned.1.call-update
  342.7 90.6 %reduce-scatter.8.cloned.1.call-done = f32[8,1024]{1,0:T(8,128)} async-done(((f32[256,1024]{1,0:T(8,128)}), f32[8,1024]{1,0:T(8,128)}) %reduce-scatter.8.cloned.1.call-update) | async-done | bytes 32784 | tf_op jit(solution)/shard_map/reduce_scatter | solution.py:153
  433.3 0.0 copy-done.8
  433.3 1.4 add_convert_fusion
  (25 shorter events, 0.1 us)
Async XLA Ops:
  6.5 114.9 %copy-start = (bf16[8,1,1024,128]{3,2,1,0:T(8,128)(2,1)S(1)}, bf16[8,1,1024,128]{3,2,1,0:T(8,128)(2,1)}, u32[]{:S(2)}) copy-start(bf16[8,1,1024,128]{3,2,1,0:T(8,128)(2,1)} %param.21) | copy-start | bytes 6291460
  6.5 25.8 %copy-start.4 = (bf16[256,128]{1,0:T(8,128)(2,1)S(1)}, bf16[256,128]{1,0:T(8,128)(2,1)}, u32[]{:S(2)}) copy-start(bf16[256,128]{1,0:T(8,128)(2,1)} %param.19) | copy-start | bytes 196612
  6.5 26.0 %copy-start.5 = (bf16[256,128]{1,0:T(8,128)(2,1)S(1)}, bf16[256,128]{1,0:T(8,128)(2,1)}, u32[]{:S(2)}) copy-start(bf16[256,128]{1,0:T(8,128)(2,1)} %param.18) | copy-start | bytes 196612
  6.5 112.8 %reduce-scatter.4.cloned.1.call-start = ((), (), s32[]{:S(2)}) async-start(), calls=%async_computation.6 | async-start | bytes 1351680 | tf_op jit(solution)/shard_map/reduce_scatter | solution.py:100
  32.6 1.5 copy-start.9
  34.0 185.6 %reduce-scatter.6.cloned.1.call-start = ((), (), s32[]{:S(2)}) async-start(), calls=%async_computation.7 | async-start | bytes 294912 | tf_op jit(solution)/shard_map/reduce_scatter | solution.py:136
  119.4 3.8 copy-start.1
  122.2 45.5 %copy-start.3 = (bf16[1024,256]{1,0:T(8,128)(2,1)S(1)}, bf16[1024,256]{1,0:T(8,128)(2,1)}, u32[]{:S(2)}) copy-start(bf16[1024,256]{1,0:T(8,128)(2,1)} %param.20) | copy-start | bytes 1572868
  123.1 62.8 %copy-start.2 = (bf16[8,8192]{1,0:T(8,128)(2,1)S(1)}, bf16[8,8192]{1,0:T(8,128)(2,1)}, u32[]{:S(2)}) copy-start(bf16[8,8192]{1,0:T(8,128)(2,1)} %param.15) | copy-start | bytes 393220
  185.9 150.7 %all-reduce.2.cloned.1.call-start = ((), (), s32[]{:S(2)}) async-start(), calls=%async_computation.8 | async-start | bytes 4194304 | tf_op jit(solution)/shard_map/psum | solution.py:150
  251.5 0.7 copy-start.6
  251.5 0.7 copy-start.7
  251.5 85.1 %copy-start.10 = (f32[2048]{0:T(1024)S(1)}, f32[2048]{0:T(1024)}, u32[]{:S(2)}) copy-start(f32[2048]{0:T(1024)} %param.25) | copy-start | bytes 24580
  251.5 181.8 %reduce-scatter.8.cloned.1.call-start = ((), (), s32[]{:S(2)}) async-start(), calls=%async_computation.9 | async-start | bytes 1081344 | tf_op jit(solution)/shard_map/reduce_scatter | solution.py:153
  336.6 96.7 %copy-start.8 = (f32[1024]{0:T(1024)S(1)}, f32[1024]{0:T(1024)}, u32[]{:S(2)}) copy-start(f32[1024]{0:T(1024)} %param.27) | copy-start | bytes 12292
Sparse Core Ops, SparseCore 0:
  34.1 85.2 reduce-scatter.3
  186.0 33.5 reduce-scatter.5
  251.7 84.8 all-reduce.1
  342.9 90.3 reduce-scatter.7
